TPU v7x, 128 devices: a whole 4x4x4 slice. The times are simulated.
128 devices in a mesh: expert: 16 (over y, x), etp: 8 (over z, core).
Axes of the slice: x: 4, y: 4, z: 4, core: 2. Of those that a mesh axis runs over, the one named last changes fastest.
Arguments:
- tokens: bfloat16 [2048, 2048], P('expert'), may hold values from -6 to 6
- out_grad: bfloat16 [2048, 2048], P('expert'), may hold values from -6 to 6
- routes: int32 [2048, 2], P('expert'), may hold values from 0 to 15, as said below
- combine_weights: float32 [2048, 2], P('expert'), may hold values from 0.2 to 1
- w_gate: bfloat16 [16, 2048, 7168], P('expert', None, 'etp'), may hold values from -0.125 to 0.125
- w_up: bfloat16 [16, 2048, 7168], P('expert', None, 'etp'), may hold values from -0.125 to 0.125
- w_down: bfloat16 [16, 7168, 2048], P('expert', 'etp'), may hold values from -0.0625 to 0.0625
Outputs:
- mixed: bfloat16 [2048, 2048], P('expert')
- tokens_grad: bfloat16 [2048, 2048], P('expert')
- combine_grad: float32 [2048, 2], P('expert')
- gate_weight_grad: bfloat16 [16, 2048, 7168], P('expert', None, 'etp')
- up_weight_grad: bfloat16 [16, 2048, 7168], P('expert', None, 'etp')
- down_weight_grad: bfloat16 [16, 7168, 2048], P('expert', 'etp')
Inputs may be any that keep to these rules, and one draw needn't show every extreme that they name: `routes`: each token names two different experts. No expert is named by more than 32 tokens of one group of 128 consecutive tokens, and one expert, the same in every group, is named by exactly 32 tokens of each group.
All inputs are finite; a program needn't handle non-finite values.
Results may differ from a plain program's by a relative error of at most 0.02.
Values may be sent and summed in bfloat16 or wider, within the bound.
No kernel may reach another device: no remote copies, remote signals or barrier semaphores. Data moves between devices by JAX's collectives and lax.ppermute only.
A program may use at most 128 MiB of HBM per device.

v0:
```python
import jax
import jax.numpy as jnp
from jax import lax
from jax.sharding import PartitionSpec as P

TOP = 2


def contract_last(left, right):
    return lax.dot_general(
        left, right, (((1,), (1,)), ((), ())), preferred_element_type=jnp.float32
    )


def contract_first(left, right):
    return lax.dot_general(
        left, right, (((0,), (0,)), ((), ())), preferred_element_type=jnp.float32
    )


def select_rows(selector, table):
    return jnp.dot(selector.astype(table.dtype), table, preferred_element_type=jnp.float32)


def expert_pass(rows_in, rows_grad, gate_w, up_w, down_w):
    gate_pre = jnp.dot(rows_in, gate_w, preferred_element_type=jnp.float32)
    up_pre = jnp.dot(rows_in, up_w, preferred_element_type=jnp.float32)
    gate_sig = jax.nn.sigmoid(gate_pre)
    swish = gate_pre * gate_sig
    hidden = (swish * up_pre).astype(jnp.bfloat16)
    out_part = jnp.dot(hidden, down_w, preferred_element_type=jnp.float32)
    hidden_grad = contract_last(rows_grad, down_w)
    down_grad = contract_first(hidden, rows_grad).astype(jnp.bfloat16)
    gate_grad = (hidden_grad * up_pre * gate_sig * (1.0 + gate_pre * (1.0 - gate_sig))).astype(
        jnp.bfloat16
    )
    up_grad = (hidden_grad * swish).astype(jnp.bfloat16)
    gate_weight_grad = contract_first(rows_in, gate_grad).astype(jnp.bfloat16)
    up_weight_grad = contract_first(rows_in, up_grad).astype(jnp.bfloat16)
    input_part = contract_last(gate_grad, gate_w) + contract_last(up_grad, up_w)
    return (out_part, input_part, gate_weight_grad, up_weight_grad, down_grad)


SLOT_OF = ((0, 1), (2, 3), (4, 7), (6, 5))


def etp_perms(split_count):
    ring = split_count // 2
    swap = [(i, i ^ 1) for i in range(split_count)]
    onward = [(i, ((i // 2 + 1 - 2 * (i % 2)) % ring) * 2 + i % 2) for i in range(split_count)]
    backward = [(target, source) for source, target in onward]
    return swap, onward, backward


def etp_gather(unit, split_count):
    swap, onward, _ = etp_perms(split_count)
    chip = jnp.stack([unit, lax.ppermute(unit, "etp", swap)], axis=1)
    first = lax.ppermute(chip, "etp", onward)
    second = lax.ppermute(first[:, 0], "etp", onward)
    held = jnp.concatenate([first, second[:, None]], axis=1)
    other = lax.ppermute(held, "etp", swap)
    return jnp.concatenate([chip, held, other], axis=1)


def etp_reduce(part, split_count):
    swap, _, backward = etp_perms(split_count)

    def send(value, perm):
        return lax.ppermute(value.astype(jnp.bfloat16), "etp", perm).astype(jnp.float32)

    held = part[2:5] + send(part[5:8], swap)
    near = held[0] + send(held[2], backward)
    chip = part[0:2] + send(jnp.stack([near, held[1]], axis=0), backward)
    return chip[0] + send(chip[1], swap)


def shards(tokens, out_grad, routes, combine_weights, w_gate, w_up, w_down):
    expert_count = lax.axis_size("expert")
    split_count = lax.axis_size("etp")
    ring = split_count // 2
    me = lax.axis_index("etp")
    my_z = me // 2
    my_core = me % 2
    token_count, features = tokens.shape
    capacity = token_count // 4
    per_split = capacity // split_count
    pair_count = token_count * TOP

    flat_routes = routes.reshape(pair_count)
    expert_hot = (flat_routes[:, None] == jnp.arange(expert_count, dtype=jnp.int32)[None, :]).astype(
        jnp.int32
    )
    before = jnp.cumsum(expert_hot, axis=0) - expert_hot
    slots = jnp.sum(before * expert_hot, axis=1)

    mine = (slots // per_split) == me
    local_place = jnp.where(mine, flat_routes * per_split + slots % per_split, -1)
    place_count = expert_count * per_split
    pick = local_place[None, :] == jnp.arange(place_count, dtype=jnp.int32)[:, None]
    pick_tokens = jnp.any(pick.reshape(place_count, token_count, TOP), axis=2)

    scaled_grad = (combine_weights[:, :, None] * out_grad.astype(jnp.float32)[:, None, :]).astype(
        jnp.bfloat16
    )
    send_rows = select_rows(pick_tokens, tokens).astype(jnp.bfloat16)
    send_grad = select_rows(pick, scaled_grad.reshape(pair_count, features)).astype(jnp.bfloat16)
    send = jnp.concatenate(
        [
            send_rows.reshape(expert_count, per_split, features),
            send_grad.reshape(expert_count, per_split, features),
        ],
        axis=1,
    )
    recv = lax.all_to_all(send, "expert", split_axis=0, concat_axis=0, tiled=True)
    recv = recv.reshape(expert_count, 2, per_split, features).transpose(1, 0, 2, 3)
    gathered = etp_gather(recv.reshape(2, place_count, features), split_count)
    row_total = split_count * place_count
    rows_in = gathered[0].reshape(row_total, features)
    rows_grad = gathered[1].reshape(row_total, features)

    out_part, input_part, gate_weight_grad, up_weight_grad, down_weight_grad = expert_pass(
        rows_in, rows_grad, w_gate[0], w_up[0], w_down[0]
    )
    block = (split_count, 1, place_count, features)
    sums = etp_reduce(
        jnp.concatenate(
            [
                out_part.astype(jnp.bfloat16).astype(jnp.float32).reshape(block),
                input_part.astype(jnp.bfloat16).astype(jnp.float32).reshape(block),
            ],
            axis=1,
        ),
        split_count,
    ).astype(jnp.bfloat16)
    back = jnp.concatenate(
        [
            sums[0].reshape(expert_count, per_split, features),
            sums[1].reshape(expert_count, per_split, features),
        ],
        axis=1,
    )
    back = lax.all_to_all(back, "expert", split_axis=0, concat_axis=0, tiled=True)
    back = back.reshape(expert_count, 2, per_split, features).transpose(1, 0, 2, 3)
    tables = etp_gather(back.reshape(2, place_count, features), split_count)
    out_table = tables[0].reshape(row_total, features)
    input_table = tables[1].reshape(row_total, features)

    source = slots // per_split
    step = 2 * my_core - 1
    ring_offset = ((source // 2 - my_z) * step) % ring
    slot_of = jnp.array(SLOT_OF, dtype=jnp.int32)[ring_offset, (source % 2) ^ my_core]
    table_row = (slot_of * expert_count + flat_routes) * per_split + slots % per_split
    gather = table_row[:, None] == jnp.arange(row_total, dtype=jnp.int32)[None, :]
    out_pairs = select_rows(gather, out_table).reshape(token_count, TOP, features)
    input_pairs = select_rows(gather, input_table).reshape(token_count, TOP, features)
    grad_values = out_grad.astype(jnp.float32)
    mixed = jnp.sum(combine_weights[:, :, None] * out_pairs, axis=1).astype(jnp.bfloat16)
    combine_grad = jnp.sum(grad_values[:, None, :] * out_pairs, axis=2)
    tokens_grad = jnp.sum(input_pairs, axis=1).astype(jnp.bfloat16)
    return (
        mixed,
        tokens_grad,
        combine_grad,
        gate_weight_grad[None],
        up_weight_grad[None],
        down_weight_grad[None],
    )


def solution(mesh):
    return jax.shard_map(
        shards,
        mesh=mesh,
        in_specs=(
            P("expert", None),
            P("expert", None),
            P("expert", None),
            P("expert", None),
            P("expert", None, "etp"),
            P("expert", None, "etp"),
            P("expert", "etp", None),
        ),
        out_specs=(
            P("expert", None),
            P("expert", None),
            P("expert", None),
            P("expert", None, "etp"),
            P("expert", None, "etp"),
            P("expert", "etp", None),
        ),
        check_vma=False,
    )
```

profile of v0, /device:TPU:1, one launch (start us, length us, event | category | flops | bytes accessed | tf_op | source)
XLA Modules:
  0.0 203.8 jit_solution(13351014722433100755)
XLA Ops:
  7.8 2.4 %mul.116 = f32[256,2048]{1,0:T(8,128)} reshape(f32[128,2,2048]{2,1,0:T(2,128)S(1)} %mul.115.clone) | data formatting | bytes 4194304 | tf_op jit(solution)/shard_map/mul | solution.py:102
  12.8 17.9 %all_to_all.10 = bf16[16,8,2048]{2,1,0:T(8,128)(2,1)S(1)} all-to-all(bf16[16,8,2048]{2,1,0:T(8,128)(2,1)S(1)} %pad_maximum_fusion.6), channel_id=1, replica_groups=mesh['expert'=16,'etp'=8] {'expert'}, dimensions={0} | all-to-all | bytes 1048576 | tf_op jit(solution)/shard_map/all_to_all | solution.py:114
  36.6 3.8 %collective-permute-start.1 = (bf16[2,2,64,2048]{3,0,2,1:T(2,128)(2,1)S(1)}, bf16[2,2,64,2048]{3,0,2,1:T(2,128)(2,1)S(1)}, u32[]{:S(2)}, u32[]{:S(2)}) collective-permute-start(bf16[2,2,64,2048]{3,0,2,1:T(2,128)(2,1)S(1)} %pad_maximum_fusion.3), channel_id=1, source_target_pairs={{0,2},{1,7},{2,4},{3,1},{4,6},{5,3},{6,0},{7,5},{8,10},{9,15},{10,... | collective-permute-start | bytes 3145736 | tf_op jit(solution)/shard_map/ppermute | solution.py:58
  40.4 11.7 %collective-permute-done.1 = bf16[2,2,64,2048]{3,0,2,1:T(2,128)(2,1)S(1)} collective-permute-done((bf16[2,2,64,2048]{3,0,2,1:T(2,128)(2,1)S(1)}, bf16[2,2,64,2048]{3,0,2,1:T(2,128)(2,1)S(1)}, u32[]{:S(2)}, u32[]{:S(2)}) %collective-permute-start.1) | collective-permute-done | bytes 1048608 | tf_op jit(solution)/shard_map/ppermute | solution.py:58
  52.6 3.2 %collective-permute-start.2 = (bf16[2,64,2048]{2,0,1:T(2,128)(2,1)S(1)}, bf16[2,64,2048]{2,0,1:T(2,128)(2,1)S(1)}, u32[]{:S(2)}, u32[]{:S(2)}) collective-permute-start(bf16[2,64,2048]{2,0,1:T(2,128)(2,1)S(1)} %slice_bitcast_fusion.4), channel_id=1, source_target_pairs={{0,2},{1,7},{2,4},{3,1},{4,6},{5,3},{6,0},{7,5},{8,10},{9,15},{10,... | collective-permute-start | bytes 1572872 | tf_op jit(solution)/shard_map/ppermute | solution.py:59
  55.7 6.1 %collective-permute-done.2 = bf16[2,64,2048]{2,0,1:T(2,128)(2,1)S(1)} collective-permute-done((bf16[2,64,2048]{2,0,1:T(2,128)(2,1)S(1)}, bf16[2,64,2048]{2,0,1:T(2,128)(2,1)S(1)}, u32[]{:S(2)}, u32[]{:S(2)}) %collective-permute-start.2) | collective-permute-done | bytes 524320 | tf_op jit(solution)/shard_map/ppermute | solution.py:59
  64.0 14.2 %collective-permute-start.3 = (bf16[2,3,64,2048]{3,0,2,1:T(2,128)(2,1)S(1)}, bf16[2,3,64,2048]{3,0,2,1:T(2,128)(2,1)S(1)}, u32[]{:S(2)}, u32[]{:S(2)}) collective-permute-start(bf16[2,3,64,2048]{3,0,2,1:T(2,128)(2,1)S(1)} %pad_maximum_fusion.1), channel_id=1, source_target_pairs={{0,1},{1,0},{2,3},{3,2},{4,5},{5,4},{6,7},{7,6},{8,9},{9,8},{10,11... | collective-permute-start | bytes 4718600 | tf_op jit(solution)/shard_map/ppermute | solution.py:61
  82.8 5.9 %fusion.49 = (bf16[1,8,64,2048]{3,0,2,1:T(2,128)(2,1)S(1)}, bf16[1,8,64,2048]{3,0,2,1:T(2,128)(2,1)S(1)}) fusion(bf16[2,8,64,2048]{3,0,2,1:T(2,128)(2,1)S(1)} %constant_dynamic-update-slice_fusion), kind=kLoop, calls=%fused_computation.125 | loop fusion | bytes 8388608 | tf_op jit(solution)/shard_map/slice | solution.py:118
  92.9 2.4 %fusion.1 = f32[512,896]{1,0:T(8,128)S(1)} fusion(bf16[512,2048]{1,0:T(8,128)(2,1)S(1)} %bitcast.146, bf16[1,896,2048]{2,1,0:T(8,128)(2,1)S(1)} %copy-done.8), kind=kOutput, calls=%fused_computation.6 | convolution fusion | flops 1879048192 | bytes 7602176 | tf_op jit(solution)/shard_map/dot_general | solution.py:10
  97.6 2.9 %multiply_convert_fusion.3 = (bf16[512,896]{1,0:T(8,128)(2,1)S(1)}, bf16[512,896]{1,0:T(8,128)(2,1)S(1)}, bf16[512,896]{1,0:T(8,128)(2,1)S(1)}) fusion(f32[512,896]{1,0:T(8,128)S(1)} %fusion.11, f32[512,896]{1,0:T(8,128)S(1)} %fusion.1, bf16[512,2048]{1,0:T(8,128)(2,1)S(1)} %bitcast.143, bf16[1,2048,896]{2,1,0:T(8,128)(2,1)S(1)} %copy-done.7), kind=kOutput, calls=%fused_computation.31 | convolution fusion | flops 1885929472 | bytes 12189696 | tf_op jit(solution)/shard_map/dot_general | solution.py:27
  100.5 2.4 %fusion.5 = f32[512,2048]{1,0:T(8,128)S(1)} fusion(bf16[512,896]{1,0:T(8,128)(2,1)S(1)} %get-tuple-element.16, bf16[1,2048,896]{2,1,0:T(8,128)(2,1)S(1)} %copy-done.7), kind=kOutput, calls=%fused_computation.10 | convolution fusion | flops 1879048192 | bytes 8781824 | tf_op jit(solution)/shard_map/dot_general | solution.py:10
  105.3 2.6 %add_convert_fusion = bf16[512,2048]{1,0:T(8,128)(2,1)S(1)} fusion(f32[512,2048]{1,0:T(8,128)S(1)} %fusion.5, bf16[512,896]{1,0:T(8,128)(2,1)S(1)} %get-tuple-element.15, bf16[1,2048,896]{2,1,0:T(8,128)(2,1)S(1)} %copy-done.9), kind=kOutput, calls=%fused_computation.5 | convolution fusion | flops 1881145344 | bytes 10878976 | tf_op jit(solution)/shard_map/dot_general | solution.py:10
  109.0 2.5 %collective-permute-done.4 = bf16[3,2,64,2048]{3,2,0,1:T(8,128)(2,1)S(1)} collective-permute-done((bf16[3,2,64,2048]{3,2,0,1:T(8,128)(2,1)S(1)}, bf16[3,2,64,2048]{3,2,0,1:T(8,128)(2,1)S(1)}, u32[]{:S(2)}, u32[]{:S(2)}) %collective-permute-start.4) | collective-permute-done | bytes 1572896 | tf_op jit(solution)/shard_map/ppermute | solution.py:69
  112.3 9.2 %collective-permute-done.5 = bf16[2,64,2048]{2,1,0:T(8,128)(2,1)S(1)} collective-permute-done((bf16[2,64,2048]{2,1,0:T(8,128)(2,1)S(1)}, bf16[2,64,2048]{2,1,0:T(8,128)(2,1)S(1)}, u32[]{:S(2)}, u32[]{:S(2)}) %collective-permute-start.5) | collective-permute-done | bytes 524320 | tf_op jit(solution)/shard_map/ppermute | solution.py:69
  121.9 14.8 %collective-permute-done.6 = bf16[2,2,64,2048]{3,2,0,1:T(8,128)(2,1)S(1)} collective-permute-done((bf16[2,2,64,2048]{3,2,0,1:T(8,128)(2,1)S(1)}, bf16[2,2,64,2048]{3,2,0,1:T(8,128)(2,1)S(1)}, u32[]{:S(2)}, u32[]{:S(2)}) %collective-permute-start.6) | collective-permute-done | bytes 1048608 | tf_op jit(solution)/shard_map/ppermute | solution.py:69
  139.8 13.5 %all_to_all.11 = bf16[16,8,2048]{2,1,0:T(8,128)(2,1)S(1)} all-to-all(bf16[16,8,2048]{2,1,0:T(8,128)(2,1)S(1)} %pad_maximum_fusion.7), channel_id=1, replica_groups=mesh['expert'=16,'etp'=8] {'expert'}, dimensions={0} | all-to-all | bytes 1048576 | tf_op jit(solution)/shard_map/all_to_all | solution.py:142
  159.3 2.9 %collective-permute-start.9 = (bf16[2,2,64,2048]{3,2,0,1:T(8,128)(2,1)S(1)}, bf16[2,2,64,2048]{3,2,0,1:T(8,128)(2,1)S(1)}, u32[]{:S(2)}, u32[]{:S(2)}) collective-permute-start(bf16[2,2,64,2048]{3,2,0,1:T(8,128)(2,1)S(1)} %pad_maximum_fusion.5), channel_id=1, source_target_pairs={{0,2},{1,7},{2,4},{3,1},{4,6},{5,3},{6,0},{7,5},{8,10},{9,15},{10,... | collective-permute-start | bytes 3145736 | tf_op jit(solution)/shard_map/ppermute | solution.py:58
  163.4 10.5 %collective-permute-done.9 = bf16[2,2,64,2048]{3,2,0,1:T(8,128)(2,1)S(1)} collective-permute-done((bf16[2,2,64,2048]{3,2,0,1:T(8,128)(2,1)S(1)}, bf16[2,2,64,2048]{3,2,0,1:T(8,128)(2,1)S(1)}, u32[]{:S(2)}, u32[]{:S(2)}) %collective-permute-start.9) | collective-permute-done | bytes 1048608 | tf_op jit(solution)/shard_map/ppermute | solution.py:58
  174.0 3.2 %collective-permute-start.10 = (bf16[2,64,2048]{2,1,0:T(8,128)(2,1)S(1)}, bf16[2,64,2048]{2,1,0:T(8,128)(2,1)S(1)}, u32[]{:S(2)}, u32[]{:S(2)}) collective-permute-start(bf16[2,64,2048]{2,1,0:T(8,128)(2,1)S(1)} %slice_bitcast_fusion.2), channel_id=1, source_target_pairs={{0,2},{1,7},{2,4},{3,1},{4,6},{5,3},{6,0},{7,5},{8,10},{9,15},{10,... | collective-permute-start | bytes 1572872 | tf_op jit(solution)/shard_map/ppermute | solution.py:59
  177.3 5.9 %collective-permute-done.10 = bf16[2,64,2048]{2,1,0:T(8,128)(2,1)S(1)} collective-permute-done((bf16[2,64,2048]{2,1,0:T(8,128)(2,1)S(1)}, bf16[2,64,2048]{2,1,0:T(8,128)(2,1)S(1)}, u32[]{:S(2)}, u32[]{:S(2)}) %collective-permute-start.10) | collective-permute-done | bytes 524320 | tf_op jit(solution)/shard_map/ppermute | solution.py:59
  183.4 3.3 %collective-permute-start.11 = (bf16[2,3,64,2048]{3,2,1,0:T(8,128)(2,1)S(1)}, bf16[2,3,64,2048]{3,2,1,0:T(8,128)(2,1)S(1)}, u32[]{:S(2)}, u32[]{:S(2)}) collective-permute-start(bf16[2,3,64,2048]{3,2,1,0:T(8,128)(2,1)S(1)} %pad_maximum_fusion.2), channel_id=1, source_target_pairs={{0,1},{1,0},{2,3},{3,2},{4,5},{5,4},{6,7},{7,6},{8,9},{9,8},{10,11... | collective-permute-start | bytes 4718600 | tf_op jit(solution)/shard_map/ppermute | solution.py:61
  186.8 4.0 %convert_bitcast_fusion = bf16[1,896,2048]{2,1,0:T(8,128)(2,1)} fusion(bf16[512,896]{1,0:T(8,128)(2,1)S(1)} %copy-done.13, bf16[512,2048]{1,0:T(8,128)(2,1)S(1)} %bitcast.147), kind=kOutput, calls=%fused_computation.18 | convolution fusion | flops 1880883200 | bytes 6684672 | tf_op jit(solution)/shard_map/dot_general | solution.py:16
  190.7 4.2 %convert_bitcast_fusion.1 = bf16[1,2048,896]{2,1,0:T(8,128)(2,1)} fusion(bf16[512,2048]{1,0:T(8,128)(2,1)S(1)} %bitcast.144, bf16[512,896]{1,0:T(8,128)(2,1)S(1)} %copy-done.11), kind=kOutput, calls=%fused_computation.19 | convolution fusion | flops 1880883200 | bytes 6684672 | tf_op jit(solution)/shard_map/dot_general | solution.py:16
  194.9 4.2 %convert_bitcast_fusion.2 = bf16[1,2048,896]{2,1,0:T(8,128)(2,1)} fusion(bf16[512,2048]{1,0:T(8,128)(2,1)S(1)} %bitcast.145, bf16[512,896]{1,0:T(8,128)(2,1)S(1)} %copy-done.15), kind=kOutput, calls=%fused_computation.20 | convolution fusion | flops 1880883200 | bytes 6684672 | tf_op jit(solution)/shard_map/dot_general | solution.py:16
  (113 shorter events, 48.3 us)
Async XLA Ops:
  0.6 5.7 %copy-start = (bf16[128,2048]{1,0:T(8,128)(2,1)S(1)}, bf16[128,2048]{1,0:T(8,128)(2,1)}, u32[]{:S(2)}) copy-start(bf16[128,2048]{1,0:T(8,128)(2,1)} %param.8) | copy-start | bytes 1572868
  0.6 6.0 %copy-start.4 = (bf16[128,2048]{1,0:T(8,128)(2,1)S(1)}, bf16[128,2048]{1,0:T(8,128)(2,1)}, u32[]{:S(2)}) copy-start(bf16[128,2048]{1,0:T(8,128)(2,1)} %param.9) | copy-start | bytes 1572868
  7.7 2.5 %copy-start.6 = (f32[128,2]{0,1:T(2,128)S(1)}, f32[128,2]{0,1:T(2,128)}, u32[]{:S(2)}) copy-start(f32[128,2]{0,1:T(2,128)} %param.11) | copy-start | bytes 3076
  31.5 3.6 %collective-permute-start = (bf16[2,64,2048]{2,0,1:T(2,128)(2,1)S(1)}, bf16[2,64,2048]{2,0,1:T(2,128)(2,1)S(1)}, u32[]{:S(2)}, u32[]{:S(2)}) collective-permute-start(bf16[2,64,2048]{2,0,1:T(2,128)(2,1)S(1)} %bitcast.139), channel_id=1, source_target_pairs={{0,1},{1,0},{2,3},{3,2},{4,5},{5,4},{6,7},{7,6},{8,9},{9,8},{10,11... | collective-permute-start | bytes 1572872 | tf_op jit(solution)/shard_map/ppermute | solution.py:57
  36.6 15.6 %collective-permute-start.1 = (bf16[2,2,64,2048]{3,0,2,1:T(2,128)(2,1)S(1)}, bf16[2,2,64,2048]{3,0,2,1:T(2,128)(2,1)S(1)}, u32[]{:S(2)}, u32[]{:S(2)}) collective-permute-start(bf16[2,2,64,2048]{3,0,2,1:T(2,128)(2,1)S(1)} %pad_maximum_fusion.3), channel_id=1, source_target_pairs={{0,2},{1,7},{2,4},{3,1},{4,6},{5,3},{6,0},{7,5},{8,10},{9,15},{10,... | collective-permute-start | bytes 3145736 | tf_op jit(solution)/shard_map/ppermute | solution.py:58
  52.6 9.3 %collective-permute-start.2 = (bf16[2,64,2048]{2,0,1:T(2,128)(2,1)S(1)}, bf16[2,64,2048]{2,0,1:T(2,128)(2,1)S(1)}, u32[]{:S(2)}, u32[]{:S(2)}) collective-permute-start(bf16[2,64,2048]{2,0,1:T(2,128)(2,1)S(1)} %slice_bitcast_fusion.4), channel_id=1, source_target_pairs={{0,2},{1,7},{2,4},{3,1},{4,6},{5,3},{6,0},{7,5},{8,10},{9,15},{10,... | collective-permute-start | bytes 1572872 | tf_op jit(solution)/shard_map/ppermute | solution.py:59
  64.0 17.2 %collective-permute-start.3 = (bf16[2,3,64,2048]{3,0,2,1:T(2,128)(2,1)S(1)}, bf16[2,3,64,2048]{3,0,2,1:T(2,128)(2,1)S(1)}, u32[]{:S(2)}, u32[]{:S(2)}) collective-permute-start(bf16[2,3,64,2048]{3,0,2,1:T(2,128)(2,1)S(1)} %pad_maximum_fusion.1), channel_id=1, source_target_pairs={{0,1},{1,0},{2,3},{3,2},{4,5},{5,4},{6,7},{7,6},{8,9},{9,8},{10,11... | collective-permute-start | bytes 4718600 | tf_op jit(solution)/shard_map/ppermute | solution.py:61
  90.1 2.8 %copy-start.8 = (bf16[1,896,2048]{2,1,0:T(8,128)(2,1)S(1)}, bf16[1,896,2048]{2,1,0:T(8,128)(2,1)}, u32[]{:S(2)}) copy-start(bf16[1,896,2048]{2,1,0:T(8,128)(2,1)} %param.14) | copy-start | bytes 11010052
  100.5 2.4 %copy-start.10 = (bf16[512,896]{1,0:T(8,128)(2,1)}, bf16[512,896]{1,0:T(8,128)(2,1)S(1)}, u32[]{:S(2)}) copy-start(bf16[512,896]{1,0:T(8,128)(2,1)S(1)} %get-tuple-element.16) | copy-start | bytes 2752516
  100.5 2.4 %copy-start.12 = (bf16[512,896]{1,0:T(8,128)(2,1)}, bf16[512,896]{1,0:T(8,128)(2,1)S(1)}, u32[]{:S(2)}) copy-start(bf16[512,896]{1,0:T(8,128)(2,1)S(1)} %get-tuple-element.14) | copy-start | bytes 2752516
  100.5 4.8 %copy-start.14 = (bf16[512,896]{1,0:T(8,128)(2,1)}, bf16[512,896]{1,0:T(8,128)(2,1)S(1)}, u32[]{:S(2)}) copy-start(bf16[512,896]{1,0:T(8,128)(2,1)S(1)} %get-tuple-element.15) | copy-start | bytes 2752516
  108.0 3.5 %collective-permute-start.4 = (bf16[3,2,64,2048]{3,2,0,1:T(8,128)(2,1)S(1)}, bf16[3,2,64,2048]{3,2,0,1:T(8,128)(2,1)S(1)}, u32[]{:S(2)}, u32[]{:S(2)}) collective-permute-start(bf16[3,2,64,2048]{3,2,0,1:T(8,128)(2,1)S(1)} %fusion.19), channel_id=1, source_target_pairs={{0,1},{1,0},{2,3},{3,2},{4,5},{5,4},{6,7},{7,6},{8,9},{9,8},{10,11... | collective-permute-start | bytes 4718600 | tf_op jit(solution)/shard_map/ppermute | solution.py:69
  112.2 9.3 %collective-permute-start.5 = (bf16[2,64,2048]{2,1,0:T(8,128)(2,1)S(1)}, bf16[2,64,2048]{2,1,0:T(8,128)(2,1)S(1)}, u32[]{:S(2)}, u32[]{:S(2)}) collective-permute-start(bf16[2,64,2048]{2,1,0:T(8,128)(2,1)S(1)} %get-tuple-element.17), channel_id=1, source_target_pairs={{2,0},{7,1},{4,2},{1,3},{6,4},{3,5},{0,6},{5,7},{10,8},{15,9},{12,... | collective-permute-start | bytes 1572872 | tf_op jit(solution)/shard_map/ppermute | solution.py:69
  121.8 14.9 %collective-permute-start.6 = (bf16[2,2,64,2048]{3,2,0,1:T(8,128)(2,1)S(1)}, bf16[2,2,64,2048]{3,2,0,1:T(8,128)(2,1)S(1)}, u32[]{:S(2)}, u32[]{:S(2)}) collective-permute-start(bf16[2,2,64,2048]{3,2,0,1:T(8,128)(2,1)S(1)} %pad_maximum_fusion.4), channel_id=1, source_target_pairs={{2,0},{7,1},{4,2},{1,3},{6,4},{3,5},{0,6},{5,7},{10,8},{15,9},{12,... | collective-permute-start | bytes 3145736 | tf_op jit(solution)/shard_map/ppermute | solution.py:69
  137.1 2.0 collective-permute-start.7
  154.6 3.5 %collective-permute-start.8 = (bf16[2,64,2048]{2,1,0:T(8,128)(2,1)}, bf16[2,64,2048]{2,1,0:T(8,128)(2,1)}, u32[]{:S(2)}, u32[]{:S(2)}) collective-permute-start(bf16[2,64,2048]{2,1,0:T(8,128)(2,1)} %reshape.359), channel_id=1, source_target_pairs={{0,1},{1,0},{2,3},{3,2},{4,5},{5,4},{6,7},{7,6},{8,9},{9,8},{10,11... | collective-permute-start | bytes 1572872 | tf_op jit(solution)/shard_map/ppermute | solution.py:57
  156.4 5.8 %copy-start.5 = (bf16[128,2048]{1,0:T(8,128)(2,1)S(1)}, bf16[128,2048]{1,0:T(8,128)(2,1)}, u32[]{:S(2)}) copy-start(bf16[128,2048]{1,0:T(8,128)(2,1)} %param.9) | copy-start | bytes 1572868
  159.3 14.6 %collective-permute-start.9 = (bf16[2,2,64,2048]{3,2,0,1:T(8,128)(2,1)S(1)}, bf16[2,2,64,2048]{3,2,0,1:T(8,128)(2,1)S(1)}, u32[]{:S(2)}, u32[]{:S(2)}) collective-permute-start(bf16[2,2,64,2048]{3,2,0,1:T(8,128)(2,1)S(1)} %pad_maximum_fusion.5), channel_id=1, source_target_pairs={{0,2},{1,7},{2,4},{3,1},{4,6},{5,3},{6,0},{7,5},{8,10},{9,15},{10,... | collective-permute-start | bytes 3145736 | tf_op jit(solution)/shard_map/ppermute | solution.py:58
  174.0 9.3 %collective-permute-start.10 = (bf16[2,64,2048]{2,1,0:T(8,128)(2,1)S(1)}, bf16[2,64,2048]{2,1,0:T(8,128)(2,1)S(1)}, u32[]{:S(2)}, u32[]{:S(2)}) collective-permute-start(bf16[2,64,2048]{2,1,0:T(8,128)(2,1)S(1)} %slice_bitcast_fusion.2), channel_id=1, source_target_pairs={{0,2},{1,7},{2,4},{3,1},{4,6},{5,3},{6,0},{7,5},{8,10},{9,15},{10,... | collective-permute-start | bytes 1572872 | tf_op jit(solution)/shard_map/ppermute | solution.py:59
  177.3 9.4 %copy-start.3 = (bf16[1,8,64,2048]{3,2,0,1:T(8,128)(2,1)S(1)}, bf16[1,8,64,2048]{3,2,0,1:T(8,128)(2,1)}, u32[]{:S(2)}) copy-start(bf16[1,8,64,2048]{3,2,0,1:T(8,128)(2,1)} %copy-done.2) | copy-start | bytes 6291460
  177.3 9.4 %copy-start.13 = (bf16[512,896]{1,0:T(8,128)(2,1)S(1)}, bf16[512,896]{1,0:T(8,128)(2,1)}, u32[]{:S(2)}) copy-start(bf16[512,896]{1,0:T(8,128)(2,1)} %copy-done.12) | copy-start | bytes 2752516
  183.4 7.3 %copy-start.11 = (bf16[512,896]{1,0:T(8,128)(2,1)S(1)}, bf16[512,896]{1,0:T(8,128)(2,1)}, u32[]{:S(2)}) copy-start(bf16[512,896]{1,0:T(8,128)(2,1)} %copy-done.10) | copy-start | bytes 2752516
  183.4 15.8 %collective-permute-start.11 = (bf16[2,3,64,2048]{3,2,1,0:T(8,128)(2,1)S(1)}, bf16[2,3,64,2048]{3,2,1,0:T(8,128)(2,1)S(1)}, u32[]{:S(2)}, u32[]{:S(2)}) collective-permute-start(bf16[2,3,64,2048]{3,2,1,0:T(8,128)(2,1)S(1)} %pad_maximum_fusion.2), channel_id=1, source_target_pairs={{0,1},{1,0},{2,3},{3,2},{4,5},{5,4},{6,7},{7,6},{8,9},{9,8},{10,11... | collective-permute-start | bytes 4718600 | tf_op jit(solution)/shard_map/ppermute | solution.py:61
  190.7 4.2 %copy-start.15 = (bf16[512,896]{1,0:T(8,128)(2,1)S(1)}, bf16[512,896]{1,0:T(8,128)(2,1)}, u32[]{:S(2)}) copy-start(bf16[512,896]{1,0:T(8,128)(2,1)} %copy-done.14) | copy-start | bytes 2752516
  (4 other events, 8.2 us)
where the time goes:
time: 206 us; the launch traced here: 204 us
  waiting for transfers between devices  66.9 us (32%)
  starting transfers between devices  35.2 us (17%)
  matrix products  32.9 us (16%)
  blocking collectives  31.4 us (15%)
  local copies, waits for them, and re-layouts  26.7 us (13%)
  other arithmetic  9.03 us (4%)
    ppermute x4, waiting for transfers between devices, send(): lax.ppermute(value.astype(jnp.bfloat16), 'etp', perm).astype(jnp.float32)  28.2 us
    ppermute x2, waiting for transfers between devices, etp_gather(): first = lax.ppermute(chip, 'etp', onward)  22.3 us
    all_to_all x1, blocking collectives, shards(): lax.all_to_all(send, 'expert', split_axis=0, concat_axis=0, tiled=True)  17.9 us
    ppermute x2, starting transfers between devices, etp_gather(): other = lax.ppermute(held, 'etp', swap)  17.5 us
    all_to_all x1, blocking collectives, shards(): lax.all_to_all(back, 'expert', split_axis=0, concat_axis=0, tiled=True)  13.5 us
    dot_general x3, matrix products, contract_first(): lax.dot_general(left, right, (((0,), (0,)), ((), ())), preferred_element_...  12.4 us
    ppermute x2, waiting for transfers between devices, etp_gather(): second = lax.ppermute(first[:, 0], 'etp', onward)  12.1 us
    unnamed x43, local copies, waits for them, and re-layouts  8.24 us
  transfers between devices with their start and end apart: 12, of which 11 were waited for; matrix products, arithmetic and copies ran while one was open for 8% of the time, Pallas kernels for 0%

commit v1 on v0

--- a/solution.py
+++ b/solution.py
@@ -41,9 +41,6 @@
     return (out_part, input_part, gate_weight_grad, up_weight_grad, down_grad)
 
 
-SLOT_OF = ((0, 1), (2, 3), (4, 7), (6, 5))
-
-
 def etp_perms(split_count):
     ring = split_count // 2
     swap = [(i, i ^ 1) for i in range(split_count)]
@@ -52,14 +49,16 @@
     return swap, onward, backward
 
 
-def etp_gather(unit, split_count):
+def etp_gather(unit, split_count, cover=None):
     swap, onward, _ = etp_perms(split_count)
     chip = jnp.stack([unit, lax.ppermute(unit, "etp", swap)], axis=1)
     first = lax.ppermute(chip, "etp", onward)
+    if cover is not None:
+        first, cover = lax.optimization_barrier((first, cover))
     second = lax.ppermute(first[:, 0], "etp", onward)
     held = jnp.concatenate([first, second[:, None]], axis=1)
     other = lax.ppermute(held, "etp", swap)
-    return jnp.concatenate([chip, held, other], axis=1)
+    return jnp.concatenate([chip, held, other], axis=1), cover
 
 
 def etp_reduce(part, split_count):
@@ -99,11 +98,9 @@
     pick = local_place[None, :] == jnp.arange(place_count, dtype=jnp.int32)[:, None]
     pick_tokens = jnp.any(pick.reshape(place_count, token_count, TOP), axis=2)
 
-    scaled_grad = (combine_weights[:, :, None] * out_grad.astype(jnp.float32)[:, None, :]).astype(
-        jnp.bfloat16
-    )
     send_rows = select_rows(pick_tokens, tokens).astype(jnp.bfloat16)
-    send_grad = select_rows(pick, scaled_grad.reshape(pair_count, features)).astype(jnp.bfloat16)
+    place_weight = jnp.sum(jnp.where(pick, combine_weights.reshape(1, pair_count), 0.0), axis=1)
+    send_grad = (place_weight[:, None] * select_rows(pick_tokens, out_grad)).astype(jnp.bfloat16)
     send = jnp.concatenate(
         [
             send_rows.reshape(expert_count, per_split, features),
@@ -113,7 +110,7 @@
     )
     recv = lax.all_to_all(send, "expert", split_axis=0, concat_axis=0, tiled=True)
     recv = recv.reshape(expert_count, 2, per_split, features).transpose(1, 0, 2, 3)
-    gathered = etp_gather(recv.reshape(2, place_count, features), split_count)
+    gathered, _ = etp_gather(recv.reshape(2, place_count, features), split_count)
     row_total = split_count * place_count
     rows_in = gathered[0].reshape(row_total, features)
     rows_grad = gathered[1].reshape(row_total, features)
@@ -141,14 +138,28 @@
     )
     back = lax.all_to_all(back, "expert", split_axis=0, concat_axis=0, tiled=True)
     back = back.reshape(expert_count, 2, per_split, features).transpose(1, 0, 2, 3)
-    tables = etp_gather(back.reshape(2, place_count, features), split_count)
+    tables, weight_grads = etp_gather(
+        back.reshape(2, place_count, features),
+        split_count,
+        (gate_weight_grad, up_weight_grad, down_weight_grad),
+    )
+    gate_weight_grad, up_weight_grad, down_weight_grad = weight_grads
     out_table = tables[0].reshape(row_total, features)
     input_table = tables[1].reshape(row_total, features)
 
     source = slots // per_split
     step = 2 * my_core - 1
     ring_offset = ((source // 2 - my_z) * step) % ring
-    slot_of = jnp.array(SLOT_OF, dtype=jnp.int32)[ring_offset, (source % 2) ^ my_core]
+    other_core = (source % 2) ^ my_core
+    slot_of = jnp.where(
+        ring_offset == 0,
+        other_core,
+        jnp.where(
+            ring_offset == 1,
+            2 + other_core,
+            jnp.where(ring_offset == 2, 4 + 3 * other_core, 6 - other_core),
+        ),
+    )
     table_row = (slot_of * expert_count + flat_routes) * per_split + slots % per_split
     gather = table_row[:, None] == jnp.arange(row_total, dtype=jnp.int32)[None, :]
     out_pairs = select_rows(gather, out_table).reshape(token_count, TOP, features)

time: 206 us -> 199 us (0.966)
  local copies, waits for them, and re-layouts: 26.7 us -> 23.3 us
  waiting for transfers between devices: 66.9 us -> 63.8 us
    ppermute x2, waiting for transfers between devices: 22.3 us -> 18.1 us  [etp_gather(): first = lax.ppermute(chip, 'etp', onward)]
    mul x5 -> x0, local copies, waits for them, and re-layouts: 3.82 us -> none  [the longest x2 3.48 us: shards(): combine_weights[:, :, None] * out_grad.astype(jnp.float32)[:, None, :]]
    ppermute x2, waiting for transfers between devices: 1.06 us -> 3.93 us  [etp_gather(): other = lax.ppermute(held, 'etp', swap)]
    gather x1 -> x0, local copies, waits for them, and re-layouts: 2.33 us -> none  [shards(): jnp.array(SLOT_OF, dtype=jnp.int32)[ring_offset, source % 2 ^ my_core]]
    unnamed x43 -> x39, local copies, waits for them, and re-layouts: 8.24 us -> 8.9 us
  transfers between devices with their start and end apart: 12 -> 12, of which waited for: 11 -> 11; matrix products, arithmetic and copies ran while one was open for 8% -> 9% of each run, Pallas kernels for 0% -> 0%
where the time goes in v1:
time: 199 us; the launch traced here: 198 us
  waiting for transfers between devices  63.8 us (32%)
  starting transfers between devices  34.9 us (18%)
  matrix products  33.8 us (17%)
  blocking collectives  31.5 us (16%)
  local copies, waits for them, and re-layouts  23.3 us (12%)
  other arithmetic  9.2 us (5%)
    ppermute x4, waiting for transfers between devices, send(): lax.ppermute(value.astype(jnp.bfloat16), 'etp', perm).astype(jnp.float32)  28.2 us
    ppermute x2, waiting for transfers between devices, etp_gather(): first = lax.ppermute(chip, 'etp', onward)  18.1 us
    all_to_all x1, blocking collectives, shards(): lax.all_to_all(send, 'expert', split_axis=0, concat_axis=0, tiled=True)  17.9 us
    ppermute x2, starting transfers between devices, etp_gather(): other = lax.ppermute(held, 'etp', swap)  17 us
    dot_general x3, matrix products, contract_first(): lax.dot_general(left, right, (((0,), (0,)), ((), ())), preferred_element_...  14 us
    all_to_all x1, blocking collectives, shards(): lax.all_to_all(back, 'expert', split_axis=0, concat_axis=0, tiled=True)  13.6 us
    ppermute x2, waiting for transfers between devices, etp_gather(): second = lax.ppermute(first[:, 0], 'etp', onward)  11.9 us
    unnamed x39, local copies, waits for them, and re-layouts  8.9 us
  transfers between devices with their start and end apart: 12, of which 11 were waited for; matrix products, arithmetic and copies ran while one was open for 9% of the time, Pallas kernels for 0%

profile of v1, /device:TPU:1, one launch (start us, length us, event | category | flops | bytes accessed | tf_op | source)
XLA Modules:
  0.0 198.1 jit_solution(17916130149835314688)
XLA Ops:
  6.8 17.9 %all_to_all.10 = bf16[16,8,2048]{2,1,0:T(8,128)(2,1)S(1)} all-to-all(bf16[16,8,2048]{2,1,0:T(8,128)(2,1)S(1)} %pad_maximum_fusion.6), channel_id=1, replica_groups=mesh['expert'=16,'etp'=8] {'expert'}, dimensions={0} | all-to-all | bytes 1048576 | tf_op jit(solution)/shard_map/all_to_all | solution.py:111
  30.6 3.8 %collective-permute-start.1 = (bf16[2,2,64,2048]{3,0,2,1:T(2,128)(2,1)S(1)}, bf16[2,2,64,2048]{3,0,2,1:T(2,128)(2,1)S(1)}, u32[]{:S(2)}, u32[]{:S(2)}) collective-permute-start(bf16[2,2,64,2048]{3,0,2,1:T(2,128)(2,1)S(1)} %pad_maximum_fusion.3), channel_id=1, source_target_pairs={{0,2},{1,7},{2,4},{3,1},{4,6},{5,3},{6,0},{7,5},{8,10},{9,15},{10,... | collective-permute-start | bytes 3145736 | tf_op jit(solution)/shard_map/ppermute | solution.py:55
  34.4 11.7 %collective-permute-done.1 = bf16[2,2,64,2048]{3,0,2,1:T(2,128)(2,1)S(1)} collective-permute-done((bf16[2,2,64,2048]{3,0,2,1:T(2,128)(2,1)S(1)}, bf16[2,2,64,2048]{3,0,2,1:T(2,128)(2,1)S(1)}, u32[]{:S(2)}, u32[]{:S(2)}) %collective-permute-start.1) | collective-permute-done | bytes 1048608 | tf_op jit(solution)/shard_map/ppermute | solution.py:55
  46.5 3.2 %collective-permute-start.2 = (bf16[2,64,2048]{2,0,1:T(2,128)(2,1)S(1)}, bf16[2,64,2048]{2,0,1:T(2,128)(2,1)S(1)}, u32[]{:S(2)}, u32[]{:S(2)}) collective-permute-start(bf16[2,64,2048]{2,0,1:T(2,128)(2,1)S(1)} %slice_bitcast_fusion.3), channel_id=1, source_target_pairs={{0,2},{1,7},{2,4},{3,1},{4,6},{5,3},{6,0},{7,5},{8,10},{9,15},{10,... | collective-permute-start | bytes 1572872 | tf_op jit(solution)/shard_map/ppermute | solution.py:58
  49.7 6.1 %collective-permute-done.2 = bf16[2,64,2048]{2,0,1:T(2,128)(2,1)S(1)} collective-permute-done((bf16[2,64,2048]{2,0,1:T(2,128)(2,1)S(1)}, bf16[2,64,2048]{2,0,1:T(2,128)(2,1)S(1)}, u32[]{:S(2)}, u32[]{:S(2)}) %collective-permute-start.2) | collective-permute-done | bytes 524320 | tf_op jit(solution)/shard_map/ppermute | solution.py:58
  58.0 14.2 %collective-permute-start.3 = (bf16[2,3,64,2048]{3,0,2,1:T(2,128)(2,1)S(1)}, bf16[2,3,64,2048]{3,0,2,1:T(2,128)(2,1)S(1)}, u32[]{:S(2)}, u32[]{:S(2)}) collective-permute-start(bf16[2,3,64,2048]{3,0,2,1:T(2,128)(2,1)S(1)} %pad_maximum_fusion.1), channel_id=1, source_target_pairs={{0,1},{1,0},{2,3},{3,2},{4,5},{5,4},{6,7},{7,6},{8,9},{9,8},{10,11... | collective-permute-start | bytes 4718600 | tf_op jit(solution)/shard_map/ppermute | solution.py:60
  76.8 5.9 %fusion.47 = (bf16[1,8,64,2048]{3,0,2,1:T(2,128)(2,1)S(1)}, bf16[1,8,64,2048]{3,0,2,1:T(2,128)(2,1)S(1)}) fusion(bf16[2,8,64,2048]{3,0,2,1:T(2,128)(2,1)S(1)} %constant_dynamic-update-slice_fusion), kind=kLoop, calls=%fused_computation.117 | loop fusion | bytes 8388608 | tf_op jit(solution)/shard_map/slice | solution.py:115
  86.8 2.4 %fusion.1 = f32[512,896]{1,0:T(8,128)S(1)} fusion(bf16[512,2048]{1,0:T(8,128)(2,1)S(1)} %bitcast.142, bf16[1,896,2048]{2,1,0:T(8,128)(2,1)S(1)} %copy-done.6), kind=kOutput, calls=%fused_computation.5 | convolution fusion | flops 1879048192 | bytes 7602176 | tf_op jit(solution)/shard_map/dot_general | solution.py:10
  91.6 3.0 %multiply_convert_fusion.2 = (bf16[512,896]{1,0:T(8,128)(2,1)S(1)}, bf16[512,896]{1,0:T(8,128)(2,1)S(1)}, bf16[512,896]{1,0:T(8,128)(2,1)S(1)}) fusion(f32[512,896]{1,0:T(8,128)S(1)} %fusion.11, f32[512,896]{1,0:T(8,128)S(1)} %fusion.1, bf16[512,2048]{1,0:T(8,128)(2,1)S(1)} %bitcast.139, bf16[1,2048,896]{2,1,0:T(8,128)(2,1)S(1)} %copy-done.5), kind=kOutput, calls=%fused_computation.30 | convolution fusion | flops 1885929472 | bytes 12189696 | tf_op jit(solution)/shard_map/dot_general | solution.py:27
  94.6 2.4 %fusion.5 = f32[512,2048]{1,0:T(8,128)S(1)} fusion(bf16[512,896]{1,0:T(8,128)(2,1)S(1)} %get-tuple-element.24, bf16[1,2048,896]{2,1,0:T(8,128)(2,1)S(1)} %copy-done.5), kind=kOutput, calls=%fused_computation.9 | convolution fusion | flops 1879048192 | bytes 8781824 | tf_op jit(solution)/shard_map/dot_general | solution.py:10
  99.3 2.6 %add_convert_fusion = bf16[512,2048]{1,0:T(8,128)(2,1)S(1)} fusion(f32[512,2048]{1,0:T(8,128)S(1)} %fusion.5, bf16[512,896]{1,0:T(8,128)(2,1)S(1)} %get-tuple-element.23, bf16[1,2048,896]{2,1,0:T(8,128)(2,1)S(1)} %copy-done.7), kind=kOutput, calls=%fused_computation.4 | convolution fusion | flops 1881145344 | bytes 10878976 | tf_op jit(solution)/shard_map/dot_general | solution.py:10
  103.1 2.5 %collective-permute-done.4 = bf16[3,2,64,2048]{3,2,0,1:T(8,128)(2,1)S(1)} collective-permute-done((bf16[3,2,64,2048]{3,2,0,1:T(8,128)(2,1)S(1)}, bf16[3,2,64,2048]{3,2,0,1:T(8,128)(2,1)S(1)}, u32[]{:S(2)}, u32[]{:S(2)}) %collective-permute-start.4) | collective-permute-done | bytes 1572896 | tf_op jit(solution)/shard_map/ppermute | solution.py:68
  106.4 9.2 %collective-permute-done.5 = bf16[2,64,2048]{2,1,0:T(8,128)(2,1)S(1)} collective-permute-done((bf16[2,64,2048]{2,1,0:T(8,128)(2,1)S(1)}, bf16[2,64,2048]{2,1,0:T(8,128)(2,1)S(1)}, u32[]{:S(2)}, u32[]{:S(2)}) %collective-permute-start.5) | collective-permute-done | bytes 524320 | tf_op jit(solution)/shard_map/ppermute | solution.py:68
  115.9 14.8 %collective-permute-done.6 = bf16[2,2,64,2048]{3,2,0,1:T(8,128)(2,1)S(1)} collective-permute-done((bf16[2,2,64,2048]{3,2,0,1:T(8,128)(2,1)S(1)}, bf16[2,2,64,2048]{3,2,0,1:T(8,128)(2,1)S(1)}, u32[]{:S(2)}, u32[]{:S(2)}) %collective-permute-start.6) | collective-permute-done | bytes 1048608 | tf_op jit(solution)/shard_map/ppermute | solution.py:68
  133.9 13.6 %all_to_all.11 = bf16[16,8,2048]{2,1,0:T(8,128)(2,1)S(1)} all-to-all(bf16[16,8,2048]{2,1,0:T(8,128)(2,1)S(1)} %pad_maximum_fusion.7), channel_id=1, replica_groups=mesh['expert'=16,'etp'=8] {'expert'}, dimensions={0} | all-to-all | bytes 1048576 | tf_op jit(solution)/shard_map/all_to_all | solution.py:139
  152.3 5.5 %convolution_convert_fusion = bf16[896,2048]{1,0:T(8,128)(2,1)} fusion(bf16[512,896]{1,0:T(8,128)(2,1)S(1)} %copy-done.11, bf16[512,2048]{1,0:T(8,128)(2,1)} %bitcast.143), kind=kOutput, calls=%fused_computation.17 | convolution fusion | flops 1880883200 | bytes 6684672 | tf_op jit(solution)/shard_map/dot_general | solution.py:16
  157.9 4.2 %convolution_convert_fusion.1 = bf16[2048,896]{1,0:T(8,128)(2,1)} fusion(bf16[512,2048]{1,0:T(8,128)(2,1)S(1)} %bitcast.140, bf16[512,896]{1,0:T(8,128)(2,1)S(1)} %copy-done.9), kind=kOutput, calls=%fused_computation.18 | convolution fusion | flops 1880883200 | bytes 6684672 | tf_op jit(solution)/shard_map/dot_general | solution.py:16
  163.5 3.1 %collective-permute-start.9 = (bf16[2,2,64,2048]{3,2,0,1:T(8,128)(2,1)S(1)}, bf16[2,2,64,2048]{3,2,0,1:T(8,128)(2,1)S(1)}, u32[]{:S(2)}, u32[]{:S(2)}) collective-permute-start(bf16[2,2,64,2048]{3,2,0,1:T(8,128)(2,1)S(1)} %pad_maximum_fusion.5), channel_id=1, source_target_pairs={{0,2},{1,7},{2,4},{3,1},{4,6},{5,3},{6,0},{7,5},{8,10},{9,15},{10,... | collective-permute-start | bytes 3145736 | tf_op jit(solution)/shard_map/ppermute | solution.py:55
  166.6 4.2 %convolution_convert_fusion.2 = bf16[2048,896]{1,0:T(8,128)(2,1)} fusion(bf16[512,2048]{1,0:T(8,128)(2,1)S(1)} %bitcast.141, bf16[512,896]{1,0:T(8,128)(2,1)S(1)} %copy-done.13), kind=kOutput, calls=%fused_computation.19 | convolution fusion | flops 1880883200 | bytes 6684672 | tf_op jit(solution)/shard_map/dot_general | solution.py:16
  172.0 6.4 %collective-permute-done.9 = bf16[2,2,64,2048]{3,2,0,1:T(8,128)(2,1)S(1)} collective-permute-done((bf16[2,2,64,2048]{3,2,0,1:T(8,128)(2,1)S(1)}, bf16[2,2,64,2048]{3,2,0,1:T(8,128)(2,1)S(1)}, u32[]{:S(2)}, u32[]{:S(2)}) %collective-permute-start.9) | collective-permute-done | bytes 1048608 | tf_op jit(solution)/shard_map/ppermute | solution.py:55
  178.4 3.2 %collective-permute-start.10 = (bf16[2,64,2048]{2,1,0:T(8,128)(2,1)S(1)}, bf16[2,64,2048]{2,1,0:T(8,128)(2,1)S(1)}, u32[]{:S(2)}, u32[]{:S(2)}) collective-permute-start(bf16[2,64,2048]{2,1,0:T(8,128)(2,1)S(1)} %slice_bitcast_fusion.4), channel_id=1, source_target_pairs={{0,2},{1,7},{2,4},{3,1},{4,6},{5,3},{6,0},{7,5},{8,10},{9,15},{10,... | collective-permute-start | bytes 1572872 | tf_op jit(solution)/shard_map/ppermute | solution.py:58
  181.9 5.8 %collective-permute-done.10 = bf16[2,64,2048]{2,1,0:T(8,128)(2,1)S(1)} collective-permute-done((bf16[2,64,2048]{2,1,0:T(8,128)(2,1)S(1)}, bf16[2,64,2048]{2,1,0:T(8,128)(2,1)S(1)}, u32[]{:S(2)}, u32[]{:S(2)}) %collective-permute-start.10) | collective-permute-done | bytes 524320 | tf_op jit(solution)/shard_map/ppermute | solution.py:58
  187.8 2.8 %collective-permute-start.11 = (bf16[2,3,64,2048]{3,2,1,0:T(8,128)(2,1)S(1)}, bf16[2,3,64,2048]{3,2,1,0:T(8,128)(2,1)S(1)}, u32[]{:S(2)}, u32[]{:S(2)}) collective-permute-start(bf16[2,3,64,2048]{3,2,1,0:T(8,128)(2,1)S(1)} %pad_maximum_fusion.2), channel_id=1, source_target_pairs={{0,1},{1,0},{2,3},{3,2},{4,5},{5,4},{6,7},{7,6},{8,9},{9,8},{10,11... | collective-permute-start | bytes 4718600 | tf_op jit(solution)/shard_map/ppermute | solution.py:60
  190.8 2.9 %collective-permute-done.11 = bf16[2,3,64,2048]{3,2,1,0:T(8,128)(2,1)S(1)} collective-permute-done((bf16[2,3,64,2048]{3,2,1,0:T(8,128)(2,1)S(1)}, bf16[2,3,64,2048]{3,2,1,0:T(8,128)(2,1)S(1)}, u32[]{:S(2)}, u32[]{:S(2)}) %collective-permute-start.11) | collective-permute-done | bytes 1572896 | tf_op jit(solution)/shard_map/ppermute | solution.py:60
  (103 shorter events, 44.9 us)
Async XLA Ops:
  0.6 5.5 %copy-start = (bf16[128,2048]{1,0:T(8,128)(2,1)S(1)}, bf16[128,2048]{1,0:T(8,128)(2,1)}, u32[]{:S(2)}) copy-start(bf16[128,2048]{1,0:T(8,128)(2,1)} %param.7) | copy-start | bytes 1572868
  25.5 3.6 %collective-permute-start = (bf16[2,64,2048]{2,0,1:T(2,128)(2,1)S(1)}, bf16[2,64,2048]{2,0,1:T(2,128)(2,1)S(1)}, u32[]{:S(2)}, u32[]{:S(2)}) collective-permute-start(bf16[2,64,2048]{2,0,1:T(2,128)(2,1)S(1)} %bitcast.135), channel_id=1, source_target_pairs={{0,1},{1,0},{2,3},{3,2},{4,5},{5,4},{6,7},{7,6},{8,9},{9,8},{10,11... | collective-permute-start | bytes 1572872 | tf_op jit(solution)/shard_map/ppermute | solution.py:54
  30.6 15.6 %collective-permute-start.1 = (bf16[2,2,64,2048]{3,0,2,1:T(2,128)(2,1)S(1)}, bf16[2,2,64,2048]{3,0,2,1:T(2,128)(2,1)S(1)}, u32[]{:S(2)}, u32[]{:S(2)}) collective-permute-start(bf16[2,2,64,2048]{3,0,2,1:T(2,128)(2,1)S(1)} %pad_maximum_fusion.3), channel_id=1, source_target_pairs={{0,2},{1,7},{2,4},{3,1},{4,6},{5,3},{6,0},{7,5},{8,10},{9,15},{10,... | collective-permute-start | bytes 3145736 | tf_op jit(solution)/shard_map/ppermute | solution.py:55
  46.5 9.3 %collective-permute-start.2 = (bf16[2,64,2048]{2,0,1:T(2,128)(2,1)S(1)}, bf16[2,64,2048]{2,0,1:T(2,128)(2,1)S(1)}, u32[]{:S(2)}, u32[]{:S(2)}) collective-permute-start(bf16[2,64,2048]{2,0,1:T(2,128)(2,1)S(1)} %slice_bitcast_fusion.3), channel_id=1, source_target_pairs={{0,2},{1,7},{2,4},{3,1},{4,6},{5,3},{6,0},{7,5},{8,10},{9,15},{10,... | collective-permute-start | bytes 1572872 | tf_op jit(solution)/shard_map/ppermute | solution.py:58
  58.0 17.2 %collective-permute-start.3 = (bf16[2,3,64,2048]{3,0,2,1:T(2,128)(2,1)S(1)}, bf16[2,3,64,2048]{3,0,2,1:T(2,128)(2,1)S(1)}, u32[]{:S(2)}, u32[]{:S(2)}) collective-permute-start(bf16[2,3,64,2048]{3,0,2,1:T(2,128)(2,1)S(1)} %pad_maximum_fusion.1), channel_id=1, source_target_pairs={{0,1},{1,0},{2,3},{3,2},{4,5},{5,4},{6,7},{7,6},{8,9},{9,8},{10,11... | collective-permute-start | bytes 4718600 | tf_op jit(solution)/shard_map/ppermute | solution.py:60
  84.0 2.8 %copy-start.6 = (bf16[1,896,2048]{2,1,0:T(8,128)(2,1)S(1)}, bf16[1,896,2048]{2,1,0:T(8,128)(2,1)}, u32[]{:S(2)}) copy-start(bf16[1,896,2048]{2,1,0:T(8,128)(2,1)} %param.13) | copy-start | bytes 11010052
  86.8 2.4 %copy-start.7 = (bf16[1,2048,896]{2,1,0:T(8,128)(2,1)S(1)}, bf16[1,2048,896]{2,1,0:T(8,128)(2,1)}, u32[]{:S(2)}) copy-start(bf16[1,2048,896]{2,1,0:T(8,128)(2,1)} %param.11) | copy-start | bytes 11010052
  89.2 2.4 %copy-start.5 = (bf16[1,2048,896]{2,1,0:T(8,128)(2,1)S(1)}, bf16[1,2048,896]{2,1,0:T(8,128)(2,1)}, u32[]{:S(2)}) copy-start(bf16[1,2048,896]{2,1,0:T(8,128)(2,1)} %param.12) | copy-start | bytes 11010052
  94.6 2.4 %copy-start.8 = (bf16[512,896]{1,0:T(8,128)(2,1)}, bf16[512,896]{1,0:T(8,128)(2,1)S(1)}, u32[]{:S(2)}) copy-start(bf16[512,896]{1,0:T(8,128)(2,1)S(1)} %get-tuple-element.24) | copy-start | bytes 2752516
  94.6 2.4 %copy-start.10 = (bf16[512,896]{1,0:T(8,128)(2,1)}, bf16[512,896]{1,0:T(8,128)(2,1)S(1)}, u32[]{:S(2)}) copy-start(bf16[512,896]{1,0:T(8,128)(2,1)S(1)} %get-tuple-element.22) | copy-start | bytes 2752516
  94.6 4.8 %copy-start.12 = (bf16[512,896]{1,0:T(8,128)(2,1)}, bf16[512,896]{1,0:T(8,128)(2,1)S(1)}, u32[]{:S(2)}) copy-start(bf16[512,896]{1,0:T(8,128)(2,1)S(1)} %get-tuple-element.23) | copy-start | bytes 2752516
  102.1 3.5 %collective-permute-start.4 = (bf16[3,2,64,2048]{3,2,0,1:T(8,128)(2,1)S(1)}, bf16[3,2,64,2048]{3,2,0,1:T(8,128)(2,1)S(1)}, u32[]{:S(2)}, u32[]{:S(2)}) collective-permute-start(bf16[3,2,64,2048]{3,2,0,1:T(8,128)(2,1)S(1)} %fusion.20), channel_id=1, source_target_pairs={{0,1},{1,0},{2,3},{3,2},{4,5},{5,4},{6,7},{7,6},{8,9},{9,8},{10,11... | collective-permute-start | bytes 4718600 | tf_op jit(solution)/shard_map/ppermute | solution.py:68
  106.3 9.3 %collective-permute-start.5 = (bf16[2,64,2048]{2,1,0:T(8,128)(2,1)S(1)}, bf16[2,64,2048]{2,1,0:T(8,128)(2,1)S(1)}, u32[]{:S(2)}, u32[]{:S(2)}) collective-permute-start(bf16[2,64,2048]{2,1,0:T(8,128)(2,1)S(1)} %get-tuple-element.25), channel_id=1, source_target_pairs={{2,0},{7,1},{4,2},{1,3},{6,4},{3,5},{0,6},{5,7},{10,8},{15,9},{12,... | collective-permute-start | bytes 1572872 | tf_op jit(solution)/shard_map/ppermute | solution.py:68
  115.8 14.9 %collective-permute-start.6 = (bf16[2,2,64,2048]{3,2,0,1:T(8,128)(2,1)S(1)}, bf16[2,2,64,2048]{3,2,0,1:T(8,128)(2,1)S(1)}, u32[]{:S(2)}, u32[]{:S(2)}) collective-permute-start(bf16[2,2,64,2048]{3,2,0,1:T(8,128)(2,1)S(1)} %pad_maximum_fusion.4), channel_id=1, source_target_pairs={{2,0},{7,1},{4,2},{1,3},{6,4},{3,5},{0,6},{5,7},{10,8},{15,9},{12,... | collective-permute-start | bytes 3145736 | tf_op jit(solution)/shard_map/ppermute | solution.py:68
  131.2 2.0 %collective-permute-start.7 = (bf16[2,64,2048]{2,1,0:T(8,128)(2,1)S(1)}, bf16[2,64,2048]{2,1,0:T(8,128)(2,1)S(1)}, u32[]{:S(2)}, u32[]{:S(2)}) collective-permute-start(bf16[2,64,2048]{2,1,0:T(8,128)(2,1)S(1)} %fusion.26), channel_id=1, source_target_pairs={{0,1},{1,0},{2,3},{3,2},{4,5},{5,4},{6,7},{7,6},{8,9},{9,8},{10,11... | collective-permute-start | bytes 1572872 | tf_op jit(solution)/shard_map/ppermute | solution.py:68
  133.8 18.5 %copy-start.11 = (bf16[512,896]{1,0:T(8,128)(2,1)S(1)}, bf16[512,896]{1,0:T(8,128)(2,1)}, u32[]{:S(2)}) copy-start(bf16[512,896]{1,0:T(8,128)(2,1)} %copy-done.10) | copy-start | bytes 2752516
  150.7 7.2 %copy-start.9 = (bf16[512,896]{1,0:T(8,128)(2,1)S(1)}, bf16[512,896]{1,0:T(8,128)(2,1)}, u32[]{:S(2)}) copy-start(bf16[512,896]{1,0:T(8,128)(2,1)} %copy-done.8) | copy-start | bytes 2752516
  150.7 11.6 %collective-permute-start.8 = (bf16[2,64,2048]{2,1,0:T(8,128)(2,1)}, bf16[2,64,2048]{2,1,0:T(8,128)(2,1)}, u32[]{:S(2)}, u32[]{:S(2)}) collective-permute-start(bf16[2,64,2048]{2,1,0:T(8,128)(2,1)} %reshape.242), channel_id=1, source_target_pairs={{0,1},{1,0},{2,3},{3,2},{4,5},{5,4},{6,7},{7,6},{8,9},{9,8},{10,11... | collective-permute-start | bytes 1572872 | tf_op jit(solution)/shard_map/ppermute | solution.py:54
  162.2 4.4 %copy-start.13 = (bf16[512,896]{1,0:T(8,128)(2,1)S(1)}, bf16[512,896]{1,0:T(8,128)(2,1)}, u32[]{:S(2)}) copy-start(bf16[512,896]{1,0:T(8,128)(2,1)} %copy-done.12) | copy-start | bytes 2752516
  163.5 14.9 %collective-permute-start.9 = (bf16[2,2,64,2048]{3,2,0,1:T(8,128)(2,1)S(1)}, bf16[2,2,64,2048]{3,2,0,1:T(8,128)(2,1)S(1)}, u32[]{:S(2)}, u32[]{:S(2)}) collective-permute-start(bf16[2,2,64,2048]{3,2,0,1:T(8,128)(2,1)S(1)} %pad_maximum_fusion.5), channel_id=1, source_target_pairs={{0,2},{1,7},{2,4},{3,1},{4,6},{5,3},{6,0},{7,5},{8,10},{9,15},{10,... | collective-permute-start | bytes 3145736 | tf_op jit(solution)/shard_map/ppermute | solution.py:55
  178.4 9.3 %collective-permute-start.10 = (bf16[2,64,2048]{2,1,0:T(8,128)(2,1)S(1)}, bf16[2,64,2048]{2,1,0:T(8,128)(2,1)S(1)}, u32[]{:S(2)}, u32[]{:S(2)}) collective-permute-start(bf16[2,64,2048]{2,1,0:T(8,128)(2,1)S(1)} %slice_bitcast_fusion.4), channel_id=1, source_target_pairs={{0,2},{1,7},{2,4},{3,1},{4,6},{5,3},{6,0},{7,5},{8,10},{9,15},{10,... | collective-permute-start | bytes 1572872 | tf_op jit(solution)/shard_map/ppermute | solution.py:58
  181.9 8.7 %copy-start.3 = (bf16[128,2048]{1,0:T(8,128)(2,1)S(1)}, bf16[128,2048]{1,0:T(8,128)(2,1)}, u32[]{:S(2)}) copy-start(bf16[128,2048]{1,0:T(8,128)(2,1)} %param.8) | copy-start | bytes 1572868
  187.8 5.8 %collective-permute-start.11 = (bf16[2,3,64,2048]{3,2,1,0:T(8,128)(2,1)S(1)}, bf16[2,3,64,2048]{3,2,1,0:T(8,128)(2,1)S(1)}, u32[]{:S(2)}, u32[]{:S(2)}) collective-permute-start(bf16[2,3,64,2048]{3,2,1,0:T(8,128)(2,1)S(1)} %pad_maximum_fusion.2), channel_id=1, source_target_pairs={{0,1},{1,0},{2,3},{3,2},{4,5},{5,4},{6,7},{7,6},{8,9},{9,8},{10,11... | collective-permute-start | bytes 4718600 | tf_op jit(solution)/shard_map/ppermute | solution.py:60
  195.9 1.7 copy-start.1
  (2 other events, 3.3 us)
